TPU v7x, 256 devices: a whole 4x4x8 slice. The times are simulated.
256 devices in a mesh: seq: 16 (over x, y), grp: 16 (over z, core).
Axes of the slice: x: 4, y: 4, z: 8, core: 2. Of those that a mesh axis runs over, the one named last changes fastest.
Arguments:
- query_rows: bfloat16 [16, 2048, 4096], P('grp', 'seq'), may hold values from -6 to 6
- key_rows: bfloat16 [16, 2048, 1024], P('grp', 'seq'), may hold values from -6 to 6
- value_rows: bfloat16 [16, 2048, 1024], P('grp', 'seq'), may hold values from -27 to 27
- doc_of_block: int32 [16, 16], P('grp'), may hold values from 0 to 3, never falling along the last dimension, each value on 1 to 8 neighbouring positions
- expert_ids: int32 [16, 2048, 2], P('grp', 'seq'), may hold values from 0 to 7, as said below
- gate_weights: float32 [16, 2048, 2], P('grp', 'seq'), may hold values from 0.1 to 0.9
- norm_gain: float32 [4096], replicated, may hold values from 0.1 to 1.9
- w_in: bfloat16 [2, 7168, 4096], P(None, ('seq', 'grp')), may hold values from -0.09375 to 0.09375
- w_down: bfloat16 [7168, 4096], P(('seq', 'grp')), may hold values from -0.0625 to 0.0625
Outputs:
- layer_out: bfloat16 [16, 2048, 4096], P('grp', 'seq')
Inputs may be any that keep to these rules, and one draw needn't show every extreme that they name: `expert_ids`: each token names 2 different experts; in each aligned block of 128 tokens along a sequence (the tokens of one device) at most 40 tokens name expert 0, and in every draw some block has exactly 40 such tokens.
All inputs are finite; a program needn't handle non-finite values.
Results may differ from a plain program's by a relative error of at most 0.014.
Values may be sent and summed in bfloat16 or wider, within the bound.
No kernel may reach another device: no remote copies, remote signals or barrier semaphores. Data moves between devices by JAX's collectives and lax.ppermute only.
A program may use at most 128 MiB of HBM per device.

v0:
```python
import math
import jax
import jax.numpy as jnp
from jax import lax
from jax.sharding import PartitionSpec as P

QH = 32
KVH = 8
HD = 128
BLK = 128
CAP = 40
EPS = 1e-05
NEG = -1e30


def project_in(gathered, piece):
    return jnp.einsum("rd,khd->krh", gathered, piece, preferred_element_type=jnp.float32)


def activate(gate_up):
    return (jax.nn.silu(gate_up[0]) * gate_up[1]).astype(jnp.bfloat16)


def add_down(hidden, piece):
    return jnp.dot(hidden, piece, preferred_element_type=jnp.float32)


def attend(query_all, key_all, value_all, token_doc, per_dev, kv_local):
    seq_length = query_all.shape[1]
    tile_rows = min(512, seq_length)
    tile_count = seq_length // tile_rows
    per_kv = per_dev // kv_local
    inv_root = 1.0 / math.sqrt(HD)
    query_split = query_all[0].reshape(seq_length, kv_local, per_kv, HD)
    key_split = key_all[0].reshape(seq_length, kv_local, HD)
    value_split = value_all[0].reshape(seq_length, kv_local, HD)
    outputs = []
    for q_index in range(tile_count):
        query_tile = query_split[q_index * tile_rows : (q_index + 1) * tile_rows]
        doc_query = token_doc[q_index * tile_rows : (q_index + 1) * tile_rows]
        allowed_row = doc_query[:, None] == token_doc[None, :]
        scores = (
            jnp.einsum("qkgd,tkd->kgqt", query_tile, key_split, preferred_element_type=jnp.float32)
            * inv_root
        )
        scores = jnp.where(allowed_row, scores, NEG)
        highest = jnp.max(scores, axis=3, keepdims=True)
        weights = jnp.exp(scores - highest)
        denom = jnp.sum(weights, axis=3, keepdims=True)
        mixed = jnp.einsum(
            "kgqt,tkd->qkgd",
            weights.astype(jnp.bfloat16),
            value_split,
            preferred_element_type=jnp.float32,
        )
        mixed = mixed / jnp.transpose(denom, (2, 0, 1, 3))
        outputs.append(mixed.reshape(tile_rows, per_dev * HD).astype(jnp.bfloat16))
    return jnp.concatenate(outputs, axis=0)[None]


def shards(
    query_rows,
    key_rows,
    value_rows,
    doc_of_block,
    expert_ids,
    gate_weights,
    norm_gain,
    w_in,
    w_down,
):
    seq_count = lax.axis_size("seq")
    tok_count = query_rows.shape[1]
    per_dev = QH // seq_count
    repeat_count = max(1, 4 // per_dev)
    kv_local = KVH * repeat_count // seq_count
    key_send = jnp.repeat(key_rows.reshape(1, tok_count, KVH, HD), repeat_count, axis=2).reshape(
        1, tok_count, KVH * repeat_count * HD
    )
    value_send = jnp.repeat(
        value_rows.reshape(1, tok_count, KVH, HD), repeat_count, axis=2
    ).reshape(1, tok_count, KVH * repeat_count * HD)
    query_all, key_all, value_all = (
        lax.all_to_all(query_rows, "seq", split_axis=2, concat_axis=1, tiled=True),
        lax.all_to_all(key_send, "seq", split_axis=2, concat_axis=1, tiled=True),
        lax.all_to_all(value_send, "seq", split_axis=2, concat_axis=1, tiled=True),
    )
    token_doc = jnp.repeat(doc_of_block[0], BLK)
    attended = attend(query_all, key_all, value_all, token_doc, per_dev, kv_local)
    attn_tokens = lax.all_to_all(attended, "seq", split_axis=1, concat_axis=2, tiled=True)
    attn_float = attn_tokens[0].astype(jnp.float32)
    spread = jnp.mean(attn_float * attn_float, axis=-1, keepdims=True)
    normed = (attn_float * lax.rsqrt(spread + EPS) * norm_gain).astype(jnp.bfloat16)
    chosen = expert_ids[0] == 0
    routed = jnp.any(chosen, axis=-1)
    gate_share = jnp.sum(jnp.where(chosen, gate_weights[0], 0.0), axis=-1)
    slot_index = jnp.cumsum(routed.astype(jnp.int32)) - 1
    onehot = (slot_index[None, :] == jnp.arange(CAP, dtype=jnp.int32)[:, None]) & routed[None, :]
    dispatched = jnp.dot(
        onehot.astype(jnp.bfloat16), normed, preferred_element_type=jnp.float32
    ).astype(jnp.bfloat16)
    gathered = lax.all_gather(dispatched, "grp", axis=0, tiled=True)
    gate_up = project_in(gathered, lax.all_gather(w_in, "seq", axis=1, tiled=True))
    hidden = activate(gate_up)
    terms = add_down(hidden, lax.all_gather(w_down, "seq", axis=0, tiled=True))
    returned = lax.psum_scatter(
        terms.astype(jnp.bfloat16), "grp", scatter_dimension=0, tiled=True
    ).astype(jnp.float32)
    picked_rows = jnp.take(returned, jnp.clip(slot_index, 0, CAP - 1), axis=0)
    expert_out = jnp.where(routed[:, None], picked_rows, 0.0)
    layer_out = attn_float + gate_share[:, None] * expert_out
    return layer_out.astype(jnp.bfloat16)[None]


def solution(mesh):
    return jax.shard_map(
        shards,
        mesh=mesh,
        in_specs=(
            P("grp", "seq", None),
            P("grp", "seq", None),
            P("grp", "seq", None),
            P("grp", None),
            P("grp", "seq", None),
            P("grp", "seq", None),
            P(),
            P(None, ("seq", "grp"), None),
            P(("seq", "grp"), None),
        ),
        out_specs=P("grp", "seq", None),
        check_vma=False,
    )
```

profile of v0, /device:TPU:2, one launch (start us, length us, event | category | flops | bytes accessed | tf_op | source)
XLA Modules:
  0.0 441.8 jit_solution(3743156761703894871)
XLA Ops:
  6.5 1.2 copy.112
  7.9 8.1 %copy.145 = bf16[1,128,2048]{1,0,2:T(2,128)(2,1)S(1)} copy(bf16[1,128,2048]{1,2,0:T(8,128)(2,1)S(1)} %bitcast.306) | data formatting | bytes 1048576 | tf_op jit(solution)/shard_map/broadcast_in_dim | solution.py:77
  16.0 0.5 broadcast.226
  16.5 11.5 %reduce.20 = bf16[2048,128]{1,0:T(8,128)(2,1)S(1)} reduce(bf16[2048,1,128]{2,1,0:T(2,128)(2,1)S(1)} %bitcast.304, bf16[]{:T(256)} %broadcast.226), dimensions={1}, to_apply=%bitcast.292.reduce_sub_computation | reduce | bytes 1048578
  28.1 0.9 reshape.333
  29.0 7.5 %all-to-all-start = ((bf16[16,2,8192]{2,1,0:T(2,128)(2,1)}), bf16[16,2,8192]{2,1,0:T(2,128)(2,1)S(1)}, u32[]{:S(2)}, u32[]{:S(2)}) async-start(bf16[16,2,8192]{2,1,0:T(2,128)(2,1)} %reshape.333), calls=%async_computation | async-start | bytes 1048576 | tf_op jit(solution)/shard_map/all_to_all | solution.py:85
  36.5 10.8 %all-gather.9.cloned.1.call-start = ((), (), s32[]{:S(2)}) async-start(), calls=%async_computation.8 | async-start | bytes 4456448 | tf_op jit(solution)/shard_map/all_gather | solution.py:105
  47.3 1.1 copy.113
  48.5 8.1 %copy.144 = bf16[1,128,2048]{1,0,2:T(2,128)(2,1)S(1)} copy(bf16[1,128,2048]{1,2,0:T(8,128)(2,1)S(1)} %bitcast.307) | data formatting | bytes 1048576 | tf_op jit(solution)/shard_map/broadcast_in_dim | solution.py:80
  56.6 11.5 %reduce.19 = bf16[2048,128]{1,0:T(8,128)(2,1)S(1)} reduce(bf16[2048,1,128]{2,1,0:T(2,128)(2,1)S(1)} %bitcast.305, bf16[]{:T(256)} %broadcast.226), dimensions={1}, to_apply=%bitcast.291.reduce_sub_computation | reduce | bytes 1048578
  68.2 0.9 reshape.331
  69.1 7.2 %all-to-all-start.2 = ((bf16[16,2,8192]{2,1,0:T(2,128)(2,1)}), bf16[16,2,8192]{2,1,0:T(2,128)(2,1)}, u32[]{:S(2)}, u32[]{:S(2)}) async-start(bf16[16,2,8192]{2,1,0:T(2,128)(2,1)} %reshape.331), calls=%async_computation.2 | async-start | bytes 1048576 | tf_op jit(solution)/shard_map/all_to_all | solution.py:86
  76.4 2.8 copy.84
  79.2 22.4 %reduce.21 = bf16[4096,128]{1,0:T(8,128)(2,1)S(1)} reduce(bf16[4096,1,128]{2,1,0:T(2,128)(2,1)S(1)} %bitcast.299, bf16[]{:T(256)} %broadcast.226), dimensions={1}, to_apply=%bitcast.272.reduce_sub_computation | reduce | bytes 2097154
  101.6 1.1 reshape.335
  102.9 7.7 %all-to-all-start.1 = ((bf16[16,2,16384]{2,1,0:T(2,128)(2,1)}), bf16[16,2,16384]{2,1,0:T(2,128)(2,1)S(1)}, u32[]{:S(2)}, u32[]{:S(2)}) async-start(bf16[16,2,16384]{2,1,0:T(2,128)(2,1)} %reshape.335), calls=%async_computation.1 | async-start | bytes 2097152 | tf_op jit(solution)/shard_map/all_to_all | solution.py:84
  110.7 3.8 broadcast_compare_fusion.3
  114.5 2.2 reshape.334
  116.8 1.0 copy.83
  117.8 2.2 reshape.332
  120.1 0.3 copy.89
  120.5 1.0 reshape.326
  121.5 3.1 all-to-all-done.1
  124.6 1.0 reshape.336
  125.9 0.1 copy.85
  126.1 3.3 fusion.10
  129.4 2.0 fusion
  131.5 2.6 fusion.59
  134.2 0.1 copy.91
  134.4 2.9 fusion.11
  137.4 2.2 fusion.2
  139.6 2.6 fusion.65
  142.3 0.1 copy.94
  142.6 2.9 fusion.12
  145.5 2.0 fusion.4
  147.6 3.3 fusion.71
  150.9 1.1 copy.102
  152.0 0.1 copy.97
  152.2 2.2 fusion.13
  154.4 2.2 fusion.6
  156.7 2.6 fusion.77
  159.5 11.7 %copy.143 = bf16[1,2048,256]{2,0,1:T(2,128)(2,1)S(1)} copy(bf16[1,2048,256]{2,1,0:T(8,128)(2,1)S(1)} %maximum_bitcast_fusion) | data formatting | bytes 2097152 | tf_op jit(solution)/shard_map/broadcast_in_dim | solution.py:58
  171.3 10.6 %reduce.22 = bf16[2048,256]{1,0:T(8,128)(2,1)S(1)} reduce(bf16[2048,1,256]{2,1,0:T(2,128)(2,1)S(1)} %bitcast.297, bf16[]{:T(256)} %broadcast.226), dimensions={1}, to_apply=%bitcast.290.reduce_sub_computation | reduce | bytes 2097154
  181.9 1.1 reshape.337
  183.0 5.6 %all-to-all-start.3 = ((bf16[16,2,16384]{2,1,0:T(2,128)(2,1)}), bf16[16,2,16384]{2,1,0:T(2,128)(2,1)S(1)}, u32[]{:S(2)}, u32[]{:S(2)}) async-start(bf16[16,2,16384]{2,1,0:T(2,128)(2,1)} %reshape.337), calls=%async_computation.3 | async-start | bytes 2097152 | tf_op jit(solution)/shard_map/all_to_all | solution.py:90
  188.8 0.2 reduce-window.4
  189.1 13.6 %all-to-all-done.3 = bf16[16,2,16384]{2,1,0:T(2,128)(2,1)S(1)} async-done(((bf16[16,2,16384]{2,1,0:T(2,128)(2,1)}), bf16[16,2,16384]{2,1,0:T(2,128)(2,1)S(1)}, u32[]{:S(2)}, u32[]{:S(2)}) %all-to-all-start.3) | async-done | bytes 1048608 | tf_op jit(solution)/shard_map/all_to_all | solution.py:90
  202.7 1.0 reshape.338
  203.7 1.2 copy.105
  205.0 1.6 copy.117
  206.6 15.4 %multiply_reduce_fusion = f32[2048]{0:T(1024)S(1)} fusion(bf16[2048,1,256]{2,1,0:T(2,128)(2,1)S(1)} %reshape.338), kind=kLoop, calls=%fused_computation.44 | loop fusion | flops 1570816 | bytes 1056768 | tf_op jit(solution)/shard_map/reduce_sum | solution.py:92
  222.1 1.1 convolution_convert_fusion.1
  223.2 0.7 all-gather.7.cloned.1.call-update
  224.0 5.1 %reshape.324 = bf16[448,4096]{1,0:T(8,128)(2,1)} reshape(bf16[16,28,4096]{2,1,0:T(8,128)(2,1)} %all-gather.9.cloned.1.call-done) | data formatting | bytes 7340032
  229.1 38.4 %all-gather.5.cloned.1.call-done = bf16[640,4096]{1,0:T(8,128)(2,1)} async-done(((bf16[40,4096]{1,0:T(8,128)(2,1)}), bf16[640,4096]{1,0:T(8,128)(2,1)}) %all-gather.5.cloned.1.call-update) | async-done | bytes 5242896 | tf_op jit(solution)/shard_map/all_gather | solution.py:102
  267.5 72.1 %all-gather.7.cloned.1.call-done = bf16[2,448,4096]{2,0,1:T(2,128)(2,1)} async-done(((bf16[2,28,4096]{2,0,1:T(2,128)(2,1)}), bf16[2,448,4096]{2,0,1:T(2,128)(2,1)}) %all-gather.7.cloned.1.call-update) | async-done | bytes 7340048 | tf_op jit(solution)/shard_map/all_gather | solution.py:103
  339.6 18.5 %fusion.35 = f32[2,640,448]{1,2,0:T(8,128)S(1)} fusion(bf16[2,448,4096]{2,0,1:T(2,128)(2,1)} %all-gather.7.cloned.1.call-done, bf16[640,4096]{1,0:T(8,128)(2,1)} %all-gather.5.cloned.1.call-done), kind=kOutput, calls=%fused_computation.49 | convolution fusion | flops 4697620480 | bytes 14876672 | tf_op jit(solution)/shard_map/rd,khd->krh/dot_general | solution.py:17
  358.2 4.8 %convolution_convert_fusion = bf16[640,4096]{1,0:T(8,128)(2,1)} fusion(bf16[448,4096]{1,0:T(8,128)(2,1)S(1)} %copy-done.4, f32[2,640,448]{1,2,0:T(8,128)S(1)} %fusion.35), kind=kOutput, calls=%fused_computation.23 | convolution fusion | flops 2353152000 | bytes 11206656 | tf_op jit(solution)/shard_map/dot_general | solution.py:25
  363.0 2.6 copy.142
  365.6 1.7 reshape.310
  367.4 60.8 %reduce-scatter.2.cloned.1.call-done = bf16[40,4096]{1,0:T(8,128)(2,1)} async-done(((bf16[640,4096]{1,0:T(8,128)(2,1)}), bf16[40,4096]{1,0:T(8,128)(2,1)}) %reduce-scatter.2.cloned.1.call-update) | async-done | bytes 327696 | tf_op jit(solution)/shard_map/reduce_scatter | solution.py:106
  428.2 1.0 convert_element_type.131
  429.2 2.6 gather_fusion
  431.7 3.1 fusion.34
  (68 shorter events, 2.2 us)
Async XLA Ops:
  6.5 69.8 %copy-start.13 = (s32[1,16]{1,0:T(1,128)S(1)}, s32[1,16]{1,0:T(1,128)}, u32[]{:S(2)}) copy-start(s32[1,16]{1,0:T(1,128)} %param.12) | copy-start | bytes 196
  6.5 69.9 %copy-start.6 = (bf16[1,128,4096]{2,1,0:T(8,128)(2,1)S(1)}, bf16[1,128,4096]{2,1,0:T(8,128)(2,1)}, u32[]{:S(2)}) copy-start(bf16[1,128,4096]{2,1,0:T(8,128)(2,1)} %param.9) | copy-start | bytes 3145732
  29.0 40.1 %all-to-all-start = ((bf16[16,2,8192]{2,1,0:T(2,128)(2,1)}), bf16[16,2,8192]{2,1,0:T(2,128)(2,1)S(1)}, u32[]{:S(2)}, u32[]{:S(2)}) async-start(bf16[16,2,8192]{2,1,0:T(2,128)(2,1)} %reshape.333), calls=%async_computation | async-start | bytes 1048576 | tf_op jit(solution)/shard_map/all_to_all | solution.py:85
  36.5 187.5 %all-gather.9.cloned.1.call-start = ((), (), s32[]{:S(2)}) async-start(), calls=%async_computation.8 | async-start | bytes 4456448 | tf_op jit(solution)/shard_map/all_gather | solution.py:105
  69.1 7.2 %copy-start.5 = (bf16[16,2,8192]{2,1,0:T(2,128)(2,1)}, bf16[16,2,8192]{2,1,0:T(2,128)(2,1)S(1)}, u32[]{:S(2)}) copy-start(bf16[16,2,8192]{2,1,0:T(2,128)(2,1)S(1)} %all-to-all-done) | copy-start | bytes 1572868
  69.1 33.8 %all-to-all-start.2 = ((bf16[16,2,8192]{2,1,0:T(2,128)(2,1)}), bf16[16,2,8192]{2,1,0:T(2,128)(2,1)}, u32[]{:S(2)}, u32[]{:S(2)}) async-start(bf16[16,2,8192]{2,1,0:T(2,128)(2,1)} %reshape.331), calls=%async_computation.2 | async-start | bytes 1048576 | tf_op jit(solution)/shard_map/all_to_all | solution.py:86
  102.9 21.7 %all-to-all-start.1 = ((bf16[16,2,16384]{2,1,0:T(2,128)(2,1)}), bf16[16,2,16384]{2,1,0:T(2,128)(2,1)S(1)}, u32[]{:S(2)}, u32[]{:S(2)}) async-start(bf16[16,2,16384]{2,1,0:T(2,128)(2,1)} %reshape.335), calls=%async_computation.1 | async-start | bytes 2097152 | tf_op jit(solution)/shard_map/all_to_all | solution.py:84
  125.8 3.6 copy-start.3
  126.1 5.3 %copy-start.8 = (bf16[2048,128,1]{0,1,2:T(8,128)(2,1)S(1)}, bf16[2048,128,1]{0,1,2:T(8,128)(2,1)}, u32[]{:S(2)}) copy-start(bf16[2048,128,1]{0,1,2:T(8,128)(2,1)} %reshape.326) | copy-start | bytes 1572868
  131.4 3.0 copy-start.2
  134.4 5.1 %copy-start.9 = (bf16[2048,128,1]{0,1,2:T(8,128)(2,1)S(1)}, bf16[2048,128,1]{0,1,2:T(8,128)(2,1)}, u32[]{:S(2)}) copy-start(bf16[2048,128,1]{0,1,2:T(8,128)(2,1)} %reshape.326) | copy-start | bytes 1572868
  139.6 3.0 copy-start.1
  142.6 5.0 %copy-start.10 = (bf16[2048,128,1]{0,1,2:T(8,128)(2,1)S(1)}, bf16[2048,128,1]{0,1,2:T(8,128)(2,1)}, u32[]{:S(2)}) copy-start(bf16[2048,128,1]{0,1,2:T(8,128)(2,1)} %reshape.326) | copy-start | bytes 1572868
  147.5 4.6 %copy-start = (pred[512,2048]{0,1:T(8,128)(4,1)S(1)}, pred[512,2048]{0,1:T(8,128)(4,1)}, u32[]{:S(2)}) copy-start(pred[512,2048]{0,1:T(8,128)(4,1)} %get-tuple-element.14) | copy-start | bytes 3145732
  147.6 4.6 %copy-start.7 = (bf16[1,16,128,128]{3,2,1,0:T(8,128)(2,1)S(1)}, bf16[1,16,128,128]{3,2,1,0:T(8,128)(2,1)}, u32[]{:S(2)}) copy-start(bf16[1,16,128,128]{3,2,1,0:T(8,128)(2,1)} %copy.83) | copy-start | bytes 1572868
  152.2 4.5 %copy-start.11 = (bf16[2048,128,1]{0,1,2:T(8,128)(2,1)S(1)}, bf16[2048,128,1]{0,1,2:T(8,128)(2,1)}, u32[]{:S(2)}) copy-start(bf16[2048,128,1]{0,1,2:T(8,128)(2,1)} %reshape.326) | copy-start | bytes 1572868
  159.3 29.3 %copy-start.14 = (s32[1,128,2]{1,2,0:T(2,128)S(1)}, s32[1,128,2]{1,2,0:T(2,128)}, u32[]{:S(2)}) copy-start(s32[1,128,2]{1,2,0:T(2,128)} %param.13) | copy-start | bytes 3076
  183.0 39.1 %copy-start.12 = (f32[4096]{0:T(1024)S(1)}, f32[4096]{0:T(1024)}, u32[]{:S(2)}) copy-start(f32[4096]{0:T(1024)} %param.15) | copy-start | bytes 49156
  183.0 19.7 %all-to-all-start.3 = ((bf16[16,2,16384]{2,1,0:T(2,128)(2,1)}), bf16[16,2,16384]{2,1,0:T(2,128)(2,1)S(1)}, u32[]{:S(2)}, u32[]{:S(2)}) async-start(bf16[16,2,16384]{2,1,0:T(2,128)(2,1)} %reshape.337), calls=%async_computation.3 | async-start | bytes 2097152 | tf_op jit(solution)/shard_map/all_to_all | solution.py:90
  188.6 78.9 %all-gather.5.cloned.1.call-start = ((), (), s32[]{:S(2)}) async-start(), calls=%async_computation.5 | async-start | bytes 5570560 | tf_op jit(solution)/shard_map/all_gather | solution.py:102
  223.2 116.4 %all-gather.7.cloned.1.call-start = ((), (), s32[]{:S(2)}) async-start(), calls=%async_computation.6 | async-start | bytes 7798784 | tf_op jit(solution)/shard_map/all_gather | solution.py:103
  223.9 204.2 %reduce-scatter.2.cloned.1.call-start = ((), (), s32[]{:S(2)}) async-start(), calls=%async_computation.7 | async-start | bytes 5570560 | tf_op jit(solution)/shard_map/reduce_scatter | solution.py:106
  339.6 18.6 %copy-start.4 = (bf16[448,4096]{1,0:T(8,128)(2,1)S(1)}, bf16[448,4096]{1,0:T(8,128)(2,1)}, u32[]{:S(2)}) copy-start(bf16[448,4096]{1,0:T(8,128)(2,1)} %reshape.324) | copy-start | bytes 11010052
  358.2 4.8 %copy-start.15 = (f32[1,128,2]{1,2,0:T(2,128)S(1)}, f32[1,128,2]{1,2,0:T(2,128)}, u32[]{:S(2)}) copy-start(f32[1,128,2]{1,2,0:T(2,128)} %param.14) | copy-start | bytes 3076
Sparse Core Ops, SparseCore 0:
  47.4 59.1 all-gather.8
  223.3 44.1 all-gather.4
  270.0 69.6 all-gather.6
  363.1 64.9 reduce-scatter.1
where the time goes:
time: 450 us; the launch traced here: 442 us
  waiting for transfers between devices  189 us (42%)
  other arithmetic  88.2 us (20%)
  local copies, waits for them, and re-layouts  64.8 us (14%)
  matrix products  46.9 us (10%)
  starting transfers between devices  38.9 us (9%)
  between operations  14.1 us (3%)
    all_gather x1, waiting for transfers between devices, shards(): lax.all_gather(w_in, 'seq', axis=1, tiled=True)  72.1 us
    reduce_scatter x1, waiting for transfers between devices, shards(): lax.psum_scatter(terms.astype(jnp.bfloat16), 'grp', scatter_dimension=0,...  60.8 us
    unnamed x4, other arithmetic  56 us
    all_gather x1, waiting for transfers between devices, shards(): gathered = lax.all_gather(dispatched, 'grp', axis=0, tiled=True)  38.4 us
    unnamed x47, local copies, waits for them, and re-layouts  21 us
    dot_general x1, matrix products, project_in(): jnp.einsum('rd,khd->krh', gathered, piece, preferred_element_type=jnp.flo...  18.5 us
    reduce_sum x2, other arithmetic, shards(): spread = jnp.mean(attn_float * attn_float, axis=-1, keepdims=True)  15.4 us
    all_to_all x1, waiting for transfers between devices, shards(): lax.all_to_all(attended, 'seq', split_axis=1, concat_axis=2, tiled=True)  13.6 us
  transfers between devices with their start and end apart: 8, of which 5 were waited for; matrix products, arithmetic and copies ran while one was open for 33% of the time, Pallas kernels for 0%

commit v1 on v0

--- a/solution.py
+++ b/solution.py
@@ -11,6 +11,22 @@
 CAP = 40
 EPS = 1e-05
 NEG = -1e30
+
+
+def pairwise_exchange(array, axis, split, join):
+    ways, here = (lax.axis_size(axis), lax.axis_index(axis))
+    width = array.shape[split] // ways
+    dims = list(array.shape)
+    dims[split] = width
+    height = dims[join]
+    dims[join] = height * ways
+    full = jnp.zeros(dims, array.dtype)
+    for mask in range(ways):
+        part = lax.dynamic_slice_in_dim(array, (here ^ mask) * width, width, axis=split)
+        if mask:
+            part = lax.ppermute(part, axis, [(d, d ^ mask) for d in range(ways)])
+        full = lax.dynamic_update_slice_in_dim(full, part, (here ^ mask) * height, axis=join)
+    return full
 
 
 def project_in(gathered, piece):
@@ -87,7 +103,7 @@
     )
     token_doc = jnp.repeat(doc_of_block[0], BLK)
     attended = attend(query_all, key_all, value_all, token_doc, per_dev, kv_local)
-    attn_tokens = lax.all_to_all(attended, "seq", split_axis=1, concat_axis=2, tiled=True)
+    attn_tokens = pairwise_exchange(attended, "seq", 1, 2)
     attn_float = attn_tokens[0].astype(jnp.float32)
     spread = jnp.mean(attn_float * attn_float, axis=-1, keepdims=True)
     normed = (attn_float * lax.rsqrt(spread + EPS) * norm_gain).astype(jnp.bfloat16)

time: 450 us -> 415 us (0.922)
  other arithmetic: 88.2 us -> 62.2 us
  local copies, waits for them, and re-layouts: 64.8 us -> 44.1 us
  starting transfers between devices: 38.9 us -> 52.5 us
    ppermute x0 -> x15, starting transfers between devices: none -> 29.8 us  [pairwise_exchange(): part = lax.ppermute(part, axis, [(d, d ^ mask) for d in range(ways)])]
    reduce_sum x2 -> x1, other arithmetic: 15.4 us -> 0.28 us  [shards(): spread = jnp.mean(attn_float * attn_float, axis=-1, keepdims=True)]
    all_to_all x1 -> x0, waiting for transfers between devices: 13.6 us -> none  [shards(): lax.all_to_all(attended, 'seq', split_axis=1, concat_axis=2, tiled=True)]
    broadcast_in_dim x1 -> x0, local copies, waits for them, and re-layouts: 11.7 us -> none  [attend(): return jnp.concatenate(outputs, axis=0)[None]]
    unnamed x4 -> x3, other arithmetic: 56 us -> 45.2 us
    all_gather x1, starting transfers between devices: 10.8 us -> 0.25 us  [shards(): terms = add_down(hidden, lax.all_gather(w_down, 'seq', axis=0, tiled=True))]
    all_to_all x1 -> x0, starting transfers between devices: 5.61 us -> none  [shards(): lax.all_to_all(attended, 'seq', split_axis=1, concat_axis=2, tiled=True)]
    convert_element_type x3 -> x0, local copies, waits for them, and re-layouts: 5.55 us -> none  [shards(): attn_float = attn_tokens[0].astype(jnp.float32)]
  transfers between devices with their start and end apart: 8 -> 22, of which waited for: 5 -> 6; matrix products, arithmetic and copies ran while one was open for 33% -> 25% of each run, Pallas kernels for 0% -> 0%
where the time goes in v1:
time: 415 us; the launch traced here: 407 us
  waiting for transfers between devices  187 us (45%)
  other arithmetic  62.2 us (15%)
  starting transfers between devices  52.5 us (13%)
  matrix products  46.3 us (11%)
  local copies, waits for them, and re-layouts  44.1 us (11%)
  between operations  14.6 us (4%)
    all_gather x1, waiting for transfers between devices, shards(): lax.all_gather(w_in, 'seq', axis=1, tiled=True)  72.1 us
    reduce_scatter x1, waiting for transfers between devices, shards(): lax.psum_scatter(terms.astype(jnp.bfloat16), 'grp', scatter_dimension=0,...  65.1 us
    unnamed x3, other arithmetic  45.2 us
    all_gather x1, waiting for transfers between devices, shards(): gathered = lax.all_gather(dispatched, 'grp', axis=0, tiled=True)  42 us
    ppermute x15, starting transfers between devices, pairwise_exchange(): part = lax.ppermute(part, axis, [(d, d ^ mask) for d in range(ways)])  29.8 us
    dot_general x1, matrix products, project_in(): jnp.einsum('rd,khd->krh', gathered, piece, preferred_element_type=jnp.flo...  18.5 us
    unnamed x44, local copies, waits for them, and re-layouts  17.2 us
    dot_general x4, matrix products, attend(): jnp.einsum('kgqt,tkd->qkgd', weights.astype(jnp.bfloat16), value_split, p...  11.8 us
  transfers between devices with their start and end apart: 22, of which 6 were waited for; matrix products, arithmetic and copies ran while one was open for 25% of the time, Pallas kernels for 0%

profile of v1, /device:TPU:2, one launch (start us, length us, event | category | flops | bytes accessed | tf_op | source)
XLA Modules:
  0.0 407.2 jit_solution(9630025417798686421)
XLA Ops:
  6.5 1.2 copy.88
  7.9 8.1 %copy.116 = bf16[1,128,2048]{1,0,2:T(2,128)(2,1)S(1)} copy(bf16[1,128,2048]{1,2,0:T(8,128)(2,1)S(1)} %bitcast.333) | data formatting | bytes 1048576 | tf_op jit(solution)/shard_map/broadcast_in_dim | solution.py:93
  16.0 0.5 broadcast.171
  16.5 11.4 %reduce.15 = bf16[2048,128]{1,0:T(8,128)(2,1)S(1)} reduce(bf16[2048,1,128]{2,1,0:T(2,128)(2,1)S(1)} %bitcast.331, bf16[]{:T(256)} %broadcast.171), dimensions={1}, to_apply=%bitcast.325.reduce_sub_computation | reduce | bytes 1048578
  28.0 0.9 reshape.286
  28.9 7.5 %all-to-all-start = ((bf16[16,2,8192]{2,1,0:T(2,128)(2,1)}), bf16[16,2,8192]{2,1,0:T(2,128)(2,1)S(1)}, u32[]{:S(2)}, u32[]{:S(2)}) async-start(bf16[16,2,8192]{2,1,0:T(2,128)(2,1)} %reshape.286), calls=%async_computation | async-start | bytes 1048576 | tf_op jit(solution)/shard_map/all_to_all | solution.py:101
  36.6 0.5 all-gather.9.cloned.1.call-update
  37.1 1.1 copy.89
  38.3 8.1 %copy.115 = bf16[1,128,2048]{1,0,2:T(2,128)(2,1)S(1)} copy(bf16[1,128,2048]{1,2,0:T(8,128)(2,1)S(1)} %bitcast.334) | data formatting | bytes 1048576 | tf_op jit(solution)/shard_map/broadcast_in_dim | solution.py:96
  46.5 11.4 %reduce.14 = bf16[2048,128]{1,0:T(8,128)(2,1)S(1)} reduce(bf16[2048,1,128]{2,1,0:T(2,128)(2,1)S(1)} %bitcast.332, bf16[]{:T(256)} %broadcast.171), dimensions={1}, to_apply=%bitcast.324.reduce_sub_computation | reduce | bytes 1048578
  57.9 0.9 reshape.284
  58.9 7.2 %all-to-all-start.2 = ((bf16[16,2,8192]{2,1,0:T(2,128)(2,1)}), bf16[16,2,8192]{2,1,0:T(2,128)(2,1)}, u32[]{:S(2)}, u32[]{:S(2)}) async-start(bf16[16,2,8192]{2,1,0:T(2,128)(2,1)} %reshape.284), calls=%async_computation.2 | async-start | bytes 1048576 | tf_op jit(solution)/shard_map/all_to_all | solution.py:102
  66.3 2.8 copy.62
  69.2 22.3 %reduce.16 = bf16[4096,128]{1,0:T(8,128)(2,1)S(1)} reduce(bf16[4096,1,128]{2,1,0:T(2,128)(2,1)S(1)} %bitcast.327, bf16[]{:T(256)} %broadcast.171), dimensions={1}, to_apply=%bitcast.311.reduce_sub_computation | reduce | bytes 2097154
  91.5 1.1 reshape.288
  93.2 7.2 %all-to-all-start.1 = ((bf16[16,2,16384]{2,1,0:T(2,128)(2,1)}), bf16[16,2,16384]{2,1,0:T(2,128)(2,1)S(1)}, u32[]{:S(2)}, u32[]{:S(2)}) async-start(bf16[16,2,16384]{2,1,0:T(2,128)(2,1)} %reshape.288), calls=%async_computation.1 | async-start | bytes 2097152 | tf_op jit(solution)/shard_map/all_to_all | solution.py:100
  100.4 0.4 all-gather.5.cloned.1.call-start
  101.0 3.8 broadcast_compare_fusion.3
  104.8 2.2 reshape.287
  107.1 1.0 copy.61
  108.1 2.2 reshape.285
  110.4 0.3 copy.67
  110.7 1.0 reshape.279
  111.8 2.8 all-to-all-done.1
  114.6 1.0 reshape.289
  116.3 3.3 fusion.10
  119.6 2.0 fusion
  121.6 2.6 fusion.61
  124.3 2.2 fusion.11
  126.5 2.2 fusion.2
  128.7 3.3 fusion.67
  132.2 2.2 fusion.12
  134.5 2.0 fusion.4
  136.5 3.3 fusion.73
  140.1 1.1 copy.80
  141.4 2.2 fusion.13
  143.7 2.2 fusion.6
  145.9 2.6 fusion.79
  149.0 0.7 collective-permute-start
  149.8 2.3 collective-permute-start.1
  152.1 1.9 collective-permute-start.2
  154.0 2.0 collective-permute-start.3
  156.0 3.1 collective-permute-start.5
  159.1 2.1 collective-permute-start.6
  161.2 2.1 collective-permute-start.7
  163.7 4.5 %collective-permute-start.9 = (bf16[1,128,256]{2,1,0:T(8,128)(2,1)S(1)}, bf16[1,128,256]{2,1,0:T(8,128)(2,1)S(1)}, u32[]{:S(2)}, u32[]{:S(2)}) collective-permute-start(bf16[1,128,256]{2,1,0:T(8,128)(2,1)S(1)} %get-tuple-element.12), channel_id=1, source_target_pairs={{0,160},{16,176},{32,128},{48,144},{64,224},{80,240},{96,192},{112... | collective-permute-start | bytes 196616 | tf_op jit(solution)/shard_map/ppermute | solution.py:27
  168.2 3.5 collective-permute-start.10
  171.7 1.1 collective-permute-start.11
  173.0 4.0 collective-permute-start.13
  176.9 2.2 collective-permute-start.14
  179.3 0.5 collective-permute-done.13
  179.8 3.6 collective-permute-done.14
  183.4 0.3 fusion.31
  183.7 1.2 convolution_convert_fusion.1
  185.0 0.7 all-gather.7.cloned.1.call-update
  185.8 5.0 %reshape.277 = bf16[448,4096]{1,0:T(8,128)(2,1)} reshape(bf16[16,28,4096]{2,1,0:T(8,128)(2,1)} %all-gather.9.cloned.1.call-done) | data formatting | bytes 7340032
  190.8 42.0 %all-gather.5.cloned.1.call-done = bf16[640,4096]{1,0:T(8,128)(2,1)} async-done(((bf16[40,4096]{1,0:T(8,128)(2,1)}), bf16[640,4096]{1,0:T(8,128)(2,1)}) %all-gather.5.cloned.1.call-update) | async-done | bytes 5242896 | tf_op jit(solution)/shard_map/all_gather | solution.py:118
  232.8 72.1 %all-gather.7.cloned.1.call-done = bf16[2,448,4096]{2,0,1:T(2,128)(2,1)} async-done(((bf16[2,28,4096]{2,0,1:T(2,128)(2,1)}), bf16[2,448,4096]{2,0,1:T(2,128)(2,1)}) %all-gather.7.cloned.1.call-update) | async-done | bytes 7340048 | tf_op jit(solution)/shard_map/all_gather | solution.py:119
  304.9 18.5 %fusion.35 = f32[2,640,448]{1,2,0:T(8,128)S(1)} fusion(bf16[2,448,4096]{2,0,1:T(2,128)(2,1)} %all-gather.7.cloned.1.call-done, bf16[640,4096]{1,0:T(8,128)(2,1)} %all-gather.5.cloned.1.call-done), kind=kOutput, calls=%fused_computation.49 | convolution fusion | flops 4697620480 | bytes 14876672 | tf_op jit(solution)/shard_map/rd,khd->krh/dot_general | solution.py:33
  323.5 4.8 %convolution_convert_fusion = bf16[640,4096]{1,0:T(8,128)(2,1)} fusion(bf16[448,4096]{1,0:T(8,128)(2,1)S(1)} %copy-done.4, f32[2,640,448]{1,2,0:T(8,128)S(1)} %fusion.35), kind=kOutput, calls=%fused_computation.23 | convolution fusion | flops 2353152000 | bytes 11206656 | tf_op jit(solution)/shard_map/dot_general | solution.py:41
  328.4 65.1 %reduce-scatter.2.cloned.1.call-done = bf16[40,4096]{1,0:T(8,128)(2,1)} async-done(((bf16[640,4096]{1,0:T(8,128)(2,1)}), bf16[40,4096]{1,0:T(8,128)(2,1)}) %reduce-scatter.2.cloned.1.call-update) | async-done | bytes 327696 | tf_op jit(solution)/shard_map/reduce_scatter | solution.py:122
  393.5 1.0 convert_element_type.90
  394.5 2.6 gather_fusion
  397.1 3.1 fusion.54
  (104 shorter events, 3.9 us)
Async XLA Ops:
  6.5 52.3 %copy-start.13 = (s32[1,128,2]{1,2,0:T(2,128)S(1)}, s32[1,128,2]{1,2,0:T(2,128)}, u32[]{:S(2)}) copy-start(s32[1,128,2]{1,2,0:T(2,128)} %param.13) | copy-start | bytes 3076
  6.5 52.3 %copy-start.12 = (s32[1,16]{1,0:T(1,128)S(1)}, s32[1,16]{1,0:T(1,128)}, u32[]{:S(2)}) copy-start(s32[1,16]{1,0:T(1,128)} %param.12) | copy-start | bytes 196
  6.5 59.8 %copy-start.6 = (bf16[1,128,4096]{2,1,0:T(8,128)(2,1)S(1)}, bf16[1,128,4096]{2,1,0:T(8,128)(2,1)}, u32[]{:S(2)}) copy-start(bf16[1,128,4096]{2,1,0:T(8,128)(2,1)} %param.9) | copy-start | bytes 3145732
  28.9 30.1 %all-to-all-start = ((bf16[16,2,8192]{2,1,0:T(2,128)(2,1)}), bf16[16,2,8192]{2,1,0:T(2,128)(2,1)S(1)}, u32[]{:S(2)}, u32[]{:S(2)}) async-start(bf16[16,2,8192]{2,1,0:T(2,128)(2,1)} %reshape.286), calls=%async_computation | async-start | bytes 1048576 | tf_op jit(solution)/shard_map/all_to_all | solution.py:101
  36.4 149.4 %all-gather.9.cloned.1.call-start = ((), (), s32[]{:S(2)}) async-start(), calls=%async_computation.7 | async-start | bytes 4456448 | tf_op jit(solution)/shard_map/all_gather | solution.py:121
  58.9 7.4 %copy-start.5 = (bf16[16,2,8192]{2,1,0:T(2,128)(2,1)}, bf16[16,2,8192]{2,1,0:T(2,128)(2,1)S(1)}, u32[]{:S(2)}) copy-start(bf16[16,2,8192]{2,1,0:T(2,128)(2,1)S(1)} %all-to-all-done) | copy-start | bytes 1572868
  58.9 34.3 %all-to-all-start.2 = ((bf16[16,2,8192]{2,1,0:T(2,128)(2,1)}), bf16[16,2,8192]{2,1,0:T(2,128)(2,1)}, u32[]{:S(2)}, u32[]{:S(2)}) async-start(bf16[16,2,8192]{2,1,0:T(2,128)(2,1)} %reshape.284), calls=%async_computation.2 | async-start | bytes 1048576 | tf_op jit(solution)/shard_map/all_to_all | solution.py:102
  93.2 21.4 %all-to-all-start.1 = ((bf16[16,2,16384]{2,1,0:T(2,128)(2,1)}), bf16[16,2,16384]{2,1,0:T(2,128)(2,1)S(1)}, u32[]{:S(2)}, u32[]{:S(2)}) async-start(bf16[16,2,16384]{2,1,0:T(2,128)(2,1)} %reshape.288), calls=%async_computation.1 | async-start | bytes 2097152 | tf_op jit(solution)/shard_map/all_to_all | solution.py:100
  100.4 132.4 %all-gather.5.cloned.1.call-start = ((), (), s32[]{:S(2)}) async-start(), calls=%async_computation.4 | async-start | bytes 5570560 | tf_op jit(solution)/shard_map/all_gather | solution.py:118
  115.8 3.8 copy-start.3
  116.3 5.3 %copy-start.8 = (bf16[2048,128,1]{0,1,2:T(8,128)(2,1)S(1)}, bf16[2048,128,1]{0,1,2:T(8,128)(2,1)}, u32[]{:S(2)}) copy-start(bf16[2048,128,1]{0,1,2:T(8,128)(2,1)} %reshape.279) | copy-start | bytes 1572868
  121.6 2.6 copy-start.2
  121.6 2.6 copy-start.7
  128.7 3.5 copy-start.1
  132.2 4.3 %copy-start.9 = (bf16[2048,128,1]{0,1,2:T(8,128)(2,1)S(1)}, bf16[2048,128,1]{0,1,2:T(8,128)(2,1)}, u32[]{:S(2)}) copy-start(bf16[2048,128,1]{0,1,2:T(8,128)(2,1)} %reshape.279) | copy-start | bytes 1572868
  136.5 3.5 copy-start.11
  136.5 4.9 %copy-start = (pred[512,2048]{0,1:T(8,128)(4,1)S(1)}, pred[512,2048]{0,1:T(8,128)(4,1)}, u32[]{:S(2)}) copy-start(pred[512,2048]{0,1:T(8,128)(4,1)} %get-tuple-element.30) | copy-start | bytes 3145732
  141.4 4.4 %copy-start.10 = (bf16[2048,128,1]{0,1,2:T(8,128)(2,1)S(1)}, bf16[2048,128,1]{0,1,2:T(8,128)(2,1)}, u32[]{:S(2)}) copy-start(bf16[2048,128,1]{0,1,2:T(8,128)(2,1)} %reshape.279) | copy-start | bytes 1572868
  148.5 35.2 %copy-start.15 = (f32[4096]{0:T(1024)S(1)}, f32[4096]{0:T(1024)}, u32[]{:S(2)}) copy-start(f32[4096]{0:T(1024)} %param.15) | copy-start | bytes 49156
  149.0 7.0 %collective-permute-start = (bf16[1,128,256]{2,1,0:T(8,128)(2,1)S(1)}, bf16[1,128,256]{2,1,0:T(8,128)(2,1)S(1)}, u32[]{:S(2)}, u32[]{:S(2)}) collective-permute-start(bf16[1,128,256]{2,1,0:T(8,128)(2,1)S(1)} %get-tuple-element.21), channel_id=1, source_target_pairs={{0,16},{16,0},{32,48},{48,32},{64,80},{80,64},{96,112},{112,96},{1... | collective-permute-start | bytes 196616 | tf_op jit(solution)/shard_map/ppermute | solution.py:27
  149.8 9.3 %collective-permute-start.1 = (bf16[1,128,256]{2,1,0:T(8,128)(2,1)S(1)}, bf16[1,128,256]{2,1,0:T(8,128)(2,1)S(1)}, u32[]{:S(2)}, u32[]{:S(2)}) collective-permute-start(bf16[1,128,256]{2,1,0:T(8,128)(2,1)S(1)} %get-tuple-element.20), channel_id=1, source_target_pairs={{0,32},{16,48},{32,0},{48,16},{64,96},{80,112},{96,64},{112,80},{1... | collective-permute-start | bytes 196616 | tf_op jit(solution)/shard_map/ppermute | solution.py:27
  152.1 9.1 %collective-permute-start.2 = (bf16[1,128,256]{2,1,0:T(8,128)(2,1)S(1)}, bf16[1,128,256]{2,1,0:T(8,128)(2,1)S(1)}, u32[]{:S(2)}, u32[]{:S(2)}) collective-permute-start(bf16[1,128,256]{2,1,0:T(8,128)(2,1)S(1)} %get-tuple-element.19), channel_id=1, source_target_pairs={{0,48},{16,32},{32,16},{48,0},{64,112},{80,96},{96,80},{112,64},{1... | collective-permute-start | bytes 196616 | tf_op jit(solution)/shard_map/ppermute | solution.py:27
  154.0 9.4 %collective-permute-start.3 = (bf16[1,128,256]{2,1,0:T(8,128)(2,1)S(1)}, bf16[1,128,256]{2,1,0:T(8,128)(2,1)S(1)}, u32[]{:S(2)}, u32[]{:S(2)}) collective-permute-start(bf16[1,128,256]{2,1,0:T(8,128)(2,1)S(1)} %get-tuple-element.18), channel_id=1, source_target_pairs={{0,64},{16,80},{32,96},{48,112},{64,0},{80,16},{96,32},{112,48},{1... | collective-permute-start | bytes 196616 | tf_op jit(solution)/shard_map/ppermute | solution.py:27
  156.0 7.7 %collective-permute-start.4 = (bf16[1,128,256]{2,1,0:T(8,128)(2,1)S(1)}, bf16[1,128,256]{2,1,0:T(8,128)(2,1)S(1)}, u32[]{:S(2)}, u32[]{:S(2)}) collective-permute-start(bf16[1,128,256]{2,1,0:T(8,128)(2,1)S(1)} %get-tuple-element.17), channel_id=1, source_target_pairs={{0,80},{16,64},{32,112},{48,96},{64,16},{80,0},{96,48},{112,32},{1... | collective-permute-start | bytes 196616 | tf_op jit(solution)/shard_map/ppermute | solution.py:27
  156.0 12.2 %collective-permute-start.5 = (bf16[1,128,256]{2,1,0:T(8,128)(2,1)S(1)}, bf16[1,128,256]{2,1,0:T(8,128)(2,1)S(1)}, u32[]{:S(2)}, u32[]{:S(2)}) collective-permute-start(bf16[1,128,256]{2,1,0:T(8,128)(2,1)S(1)} %get-tuple-element.16), channel_id=1, source_target_pairs={{0,96},{16,112},{32,64},{48,80},{64,32},{80,48},{96,0},{112,16},{1... | collective-permute-start | bytes 196616 | tf_op jit(solution)/shard_map/ppermute | solution.py:27
  159.1 12.6 %collective-permute-start.6 = (bf16[1,128,256]{2,1,0:T(8,128)(2,1)S(1)}, bf16[1,128,256]{2,1,0:T(8,128)(2,1)S(1)}, u32[]{:S(2)}, u32[]{:S(2)}) collective-permute-start(bf16[1,128,256]{2,1,0:T(8,128)(2,1)S(1)} %get-tuple-element.15), channel_id=1, source_target_pairs={{0,112},{16,96},{32,80},{48,64},{64,48},{80,32},{96,16},{112,0},{1... | collective-permute-start | bytes 196616 | tf_op jit(solution)/shard_map/ppermute | solution.py:27
  161.2 11.6 %collective-permute-start.7 = (bf16[1,128,256]{2,1,0:T(8,128)(2,1)S(1)}, bf16[1,128,256]{2,1,0:T(8,128)(2,1)S(1)}, u32[]{:S(2)}, u32[]{:S(2)}) collective-permute-start(bf16[1,128,256]{2,1,0:T(8,128)(2,1)S(1)} %get-tuple-element.14), channel_id=1, source_target_pairs={{0,128},{16,144},{32,160},{48,176},{64,192},{80,208},{96,224},{112... | collective-permute-start | bytes 196616 | tf_op jit(solution)/shard_map/ppermute | solution.py:27
  163.4 9.6 %collective-permute-start.8 = (bf16[1,128,256]{2,1,0:T(8,128)(2,1)S(1)}, bf16[1,128,256]{2,1,0:T(8,128)(2,1)S(1)}, u32[]{:S(2)}, u32[]{:S(2)}) collective-permute-start(bf16[1,128,256]{2,1,0:T(8,128)(2,1)S(1)} %get-tuple-element.13), channel_id=1, source_target_pairs={{0,144},{16,128},{32,176},{48,160},{64,208},{80,192},{96,240},{112... | collective-permute-start | bytes 196616 | tf_op jit(solution)/shard_map/ppermute | solution.py:27
  163.7 13.3 %collective-permute-start.9 = (bf16[1,128,256]{2,1,0:T(8,128)(2,1)S(1)}, bf16[1,128,256]{2,1,0:T(8,128)(2,1)S(1)}, u32[]{:S(2)}, u32[]{:S(2)}) collective-permute-start(bf16[1,128,256]{2,1,0:T(8,128)(2,1)S(1)} %get-tuple-element.12), channel_id=1, source_target_pairs={{0,160},{16,176},{32,128},{48,144},{64,224},{80,240},{96,192},{112... | collective-permute-start | bytes 196616 | tf_op jit(solution)/shard_map/ppermute | solution.py:27
  168.2 11.0 %collective-permute-start.10 = (bf16[1,128,256]{2,1,0:T(8,128)(2,1)S(1)}, bf16[1,128,256]{2,1,0:T(8,128)(2,1)S(1)}, u32[]{:S(2)}, u32[]{:S(2)}) collective-permute-start(bf16[1,128,256]{2,1,0:T(8,128)(2,1)S(1)} %get-tuple-element.11), channel_id=1, source_target_pairs={{0,176},{16,160},{32,144},{48,128},{64,240},{80,224},{96,208},{112... | collective-permute-start | bytes 196616 | tf_op jit(solution)/shard_map/ppermute | solution.py:27
  171.7 7.5 %collective-permute-start.11 = (bf16[1,128,256]{2,1,0:T(8,128)(2,1)S(1)}, bf16[1,128,256]{2,1,0:T(8,128)(2,1)S(1)}, u32[]{:S(2)}, u32[]{:S(2)}) collective-permute-start(bf16[1,128,256]{2,1,0:T(8,128)(2,1)S(1)} %get-tuple-element.10), channel_id=1, source_target_pairs={{0,192},{16,208},{32,224},{48,240},{64,128},{80,144},{96,160},{112... | collective-permute-start | bytes 196616 | tf_op jit(solution)/shard_map/ppermute | solution.py:27
  172.8 6.4 %collective-permute-start.12 = (bf16[1,128,256]{2,1,0:T(8,128)(2,1)S(1)}, bf16[1,128,256]{2,1,0:T(8,128)(2,1)S(1)}, u32[]{:S(2)}, u32[]{:S(2)}) collective-permute-start(bf16[1,128,256]{2,1,0:T(8,128)(2,1)S(1)} %get-tuple-element.9), channel_id=1, source_target_pairs={{0,208},{16,192},{32,240},{48,224},{64,144},{80,128},{96,176},{112... | collective-permute-start | bytes 196616 | tf_op jit(solution)/shard_map/ppermute | solution.py:27
  173.0 6.8 %collective-permute-start.13 = (bf16[1,128,256]{2,1,0:T(8,128)(2,1)S(1)}, bf16[1,128,256]{2,1,0:T(8,128)(2,1)S(1)}, u32[]{:S(2)}, u32[]{:S(2)}) collective-permute-start(bf16[1,128,256]{2,1,0:T(8,128)(2,1)S(1)} %get-tuple-element.8), channel_id=1, source_target_pairs={{0,224},{16,240},{32,192},{48,208},{64,160},{80,176},{96,128},{112... | collective-permute-start | bytes 196616 | tf_op jit(solution)/shard_map/ppermute | solution.py:27
  176.9 6.5 %collective-permute-start.14 = (bf16[1,128,256]{2,1,0:T(8,128)(2,1)S(1)}, bf16[1,128,256]{2,1,0:T(8,128)(2,1)S(1)}, u32[]{:S(2)}, u32[]{:S(2)}) collective-permute-start(bf16[1,128,256]{2,1,0:T(8,128)(2,1)S(1)} %get-tuple-element.7), channel_id=1, source_target_pairs={{0,240},{16,224},{32,208},{48,192},{64,176},{80,160},{96,144},{112... | collective-permute-start | bytes 196616 | tf_op jit(solution)/shard_map/ppermute | solution.py:27
  185.0 120.0 %all-gather.7.cloned.1.call-start = ((), (), s32[]{:S(2)}) async-start(), calls=%async_computation.5 | async-start | bytes 7798784 | tf_op jit(solution)/shard_map/all_gather | solution.py:119
  185.7 207.8 %reduce-scatter.2.cloned.1.call-start = ((), (), s32[]{:S(2)}) async-start(), calls=%async_computation.6 | async-start | bytes 5570560 | tf_op jit(solution)/shard_map/reduce_scatter | solution.py:122
  304.9 18.6 %copy-start.4 = (bf16[448,4096]{1,0:T(8,128)(2,1)S(1)}, bf16[448,4096]{1,0:T(8,128)(2,1)}, u32[]{:S(2)}) copy-start(bf16[448,4096]{1,0:T(8,128)(2,1)} %reshape.277) | copy-start | bytes 11010052
  323.5 4.8 %copy-start.14 = (f32[1,128,2]{1,2,0:T(2,128)S(1)}, f32[1,128,2]{1,2,0:T(2,128)}, u32[]{:S(2)}) copy-start(f32[1,128,2]{1,2,0:T(2,128)} %param.14) | copy-start | bytes 3076
Sparse Core Ops, SparseCore 0:
  39.6 59.1 all-gather.8
  185.1 47.6 all-gather.4
  235.3 69.6 all-gather.6
  328.5 64.9 reduce-scatter.1
